TPU v7x, 32 devices: a whole 2x2x4 slice. The times are simulated.
32 devices in a mesh: groups: 2 (over x), freq: 16 (over z, y, core).
Axes of the slice: x: 2, y: 2, z: 4, core: 2. Of those that a mesh axis runs over, the one named last changes fastest.
Arguments:
- encoder_input: bfloat16 [64, 2048], P(('groups', 'freq')), parts along dimension 0, may hold values from -6 to 6
- desired_responses: bfloat16 [64, 384, 512], P('groups', 'freq'), parts along dimension 0, may hold values from -6 to 6
- sample_index: int32 [64], P('groups'), parts along dimension 0, may hold values from 0 to 31, each once
- encoder_weight: bfloat16 [2048, 512], replicated, may hold values from -0.125 to 0.125
- decoder_weight: bfloat16 [512, 512], replicated, may hold values from -0.25 to 0.25
- frequency_amplitude: bfloat16 [384, 512], P('freq'), may hold values from -4 to 4
- spectral_filter_weight: float32 [2, 256], replicated, may hold values from -4 to 4
- output_weight: bfloat16 [512, 512], replicated, may hold values from -0.25 to 0.25
Outputs:
- grad_enc: float32 [4096, 512], P('groups'), parts along dimension 0
- grad_dec: float32 [1024, 512], P('groups'), parts along dimension 0
- grad_out: float32 [1024, 512], P('groups'), parts along dimension 0
- grad_filter: float32 [4, 256], P('groups'), parts along dimension 0
There are 2 independent parts, one for each index of `groups`. A program takes and returns all parts, laid end to end along the dimension named above; an argument that names none is the same for every part. Nothing has to cross between parts.
Inputs may be any that keep to these rules, and one draw needn't show every extreme that they name: sample_index names each of the 32 samples once.
All inputs are finite; a program needn't handle non-finite values.
Results may differ from a plain program's by a relative error of at most 0.0065.
Values may be sent and summed in bfloat16 or wider, within the bound.
No kernel may reach another device: no remote copies, remote signals or barrier semaphores. Data moves between devices by JAX's collectives and lax.ppermute only.
A program may use at most 128 MiB of HBM per device.

v0:
```python
import math
import jax
import jax.numpy as jnp
from jax import lax
from jax.sharding import PartitionSpec as P


def rotation_tables(antennas):
    indices = jnp.arange(antennas, dtype=jnp.int32)
    products_mod = indices[:, None] * indices[None, :] % antennas
    angle_table = products_mod.astype(jnp.float32) * (2.0 * math.pi / antennas)
    cosine_table = jnp.cos(angle_table) / math.sqrt(antennas)
    sine_table = jnp.sin(angle_table) / math.sqrt(antennas)
    forward_transform = jnp.concatenate(
        [
            jnp.concatenate([cosine_table, -sine_table], 1),
            jnp.concatenate([sine_table, cosine_table], 1),
        ],
        0,
    )
    inverse_transform = jnp.concatenate(
        [
            jnp.concatenate([cosine_table, sine_table], 1),
            jnp.concatenate([-sine_table, cosine_table], 1),
        ],
        0,
    )
    return (forward_transform.astype(jnp.bfloat16), inverse_transform.astype(jnp.bfloat16))


def decode_rows(
    mixed_in,
    wanted_lines,
    output_weight,
    spectral_filter_weight,
    forward_transform,
    inverse_transform,
    loss_scale,
):
    filter_re = spectral_filter_weight[0]
    filter_im = spectral_filter_weight[1]
    spectrum = jnp.dot(mixed_in, forward_transform, preferred_element_type=jnp.float32)
    half_width = spectrum.shape[1] // 2
    spec_re = spectrum[:, :half_width]
    spec_im = spectrum[:, half_width:]
    filtered = jnp.concatenate(
        [spec_re * filter_re - spec_im * filter_im, spec_re * filter_im + spec_im * filter_re], 1
    ).astype(jnp.bfloat16)
    mixed_back = jnp.dot(filtered, inverse_transform, preferred_element_type=jnp.float32)
    hidden = (mixed_in.astype(jnp.float32) + jax.nn.gelu(mixed_back)).astype(jnp.bfloat16)
    rebuilt = hidden.astype(jnp.float32) + jnp.dot(
        hidden, output_weight, preferred_element_type=jnp.float32
    )
    residual = loss_scale * (rebuilt - wanted_lines.astype(jnp.float32))
    residual_half = residual.astype(jnp.bfloat16)
    grad_out = lax.dot_general(
        hidden, residual_half, (((0,), (0,)), ((), ())), preferred_element_type=jnp.float32
    )
    grad_hidden = residual + lax.dot_general(
        residual_half, output_weight, (((1,), (1,)), ((), ())), preferred_element_type=jnp.float32
    )
    grad_mixed = jax.vjp(jax.nn.gelu, mixed_back)[1](grad_hidden)[0].astype(jnp.bfloat16)
    grad_filtered = lax.dot_general(
        grad_mixed, inverse_transform, (((1,), (1,)), ((), ())), preferred_element_type=jnp.float32
    )
    grad_re = grad_filtered[:, :half_width]
    grad_im = grad_filtered[:, half_width:]
    grad_filter = jnp.stack(
        [
            jnp.sum(grad_re * spec_re + grad_im * spec_im, 0),
            jnp.sum(grad_im * spec_re - grad_re * spec_im, 0),
        ]
    )
    grad_spec = jnp.concatenate(
        [grad_re * filter_re + grad_im * filter_im, grad_im * filter_re - grad_re * filter_im], 1
    ).astype(jnp.bfloat16)
    derivative_entering = grad_hidden + lax.dot_general(
        grad_spec, forward_transform, (((1,), (1,)), ((), ())), preferred_element_type=jnp.float32
    )
    return (derivative_entering, grad_out, grad_filter)


def encoder_grads(inputs_rows, codewords, latent_sums, decoder_weight):
    latent_half = latent_sums.astype(jnp.bfloat16)
    grad_dec = lax.dot_general(
        codewords, latent_half, (((0,), (0,)), ((), ())), preferred_element_type=jnp.float32
    )
    grad_codes = lax.dot_general(
        latent_half, decoder_weight, (((1,), (1,)), ((), ())), preferred_element_type=jnp.float32
    )
    grad_pre = (grad_codes * (1.0 - jnp.square(codewords.astype(jnp.float32)))).astype(jnp.bfloat16)
    grad_enc = lax.dot_general(
        inputs_rows, grad_pre, (((0,), (0,)), ((), ())), preferred_element_type=jnp.float32
    )
    return (grad_enc, grad_dec)


def local(
    encoder_input,
    desired_responses,
    sample_index,
    encoder_weight,
    decoder_weight,
    frequency_amplitude,
    spectral_filter_weight,
    output_weight,
):
    samples = sample_index.shape[0]
    sub_dev = desired_responses.shape[1]
    width = desired_responses.shape[2]
    forward_transform, inverse_transform = rotation_tables(width // 2)
    loss_scale = 1.0 / math.sqrt(samples * sub_dev * lax.axis_size("freq"))
    codes_own = jnp.tanh(
        jnp.dot(encoder_input, encoder_weight, preferred_element_type=jnp.float32)
    ).astype(jnp.bfloat16)
    all_codes = lax.all_gather(codes_own, "freq", axis=0, tiled=True)
    inverse_ids = (
        jnp.zeros((samples,), jnp.int32).at[sample_index].set(jnp.arange(samples, dtype=jnp.int32))
    )
    latent = jnp.dot(all_codes[inverse_ids], decoder_weight, preferred_element_type=jnp.float32)
    gain_row_values = frequency_amplitude.astype(jnp.float32)
    mixed_in = (latent[:, None, :] * gain_row_values[None]).astype(jnp.bfloat16).reshape(-1, width)
    wanted_lines = desired_responses.reshape(-1, width)
    derivative_entering, grad_out, grad_filter = decode_rows(
        mixed_in,
        wanted_lines,
        output_weight,
        spectral_filter_weight,
        forward_transform,
        inverse_transform,
        loss_scale,
    )
    derivative_bottleneck = jnp.einsum(
        "orm,rm->om", derivative_entering.reshape(samples, sub_dev, width), gain_row_values
    )
    enc_order = derivative_bottleneck[sample_index]
    owned_rows = lax.psum_scatter(enc_order, "freq", scatter_dimension=0, tiled=True)
    grad_enc, grad_dec = encoder_grads(encoder_input, codes_own, owned_rows, decoder_weight)
    grad_enc, grad_dec, grad_out, grad_filter = lax.psum(
        (grad_enc, grad_dec, grad_out, grad_filter), "freq"
    )
    return (grad_enc, grad_dec, grad_out, grad_filter)


def solution(mesh):
    return jax.shard_map(
        local,
        mesh=mesh,
        in_specs=(
            P(("groups", "freq"), None),
            P("groups", "freq", None),
            P("groups"),
            P(),
            P(),
            P("freq", None),
            P(),
            P(),
        ),
        out_specs=(P("groups", None), P("groups", None), P("groups", None), P("groups", None)),
        check_vma=False,
    )
```

profile of v0, /device:TPU:0, one launch (start us, length us, event | category | flops | bytes accessed | tf_op | source)
XLA Modules:
  0.0 264.4 jit_solution(11074158935546057527)
XLA Ops:
  7.2 0.0 copy-start
  7.2 0.0 copy-start.9
  7.2 0.0 copy-start.1
  7.2 0.0 all-reduce.5.cloned.1.call-start
  7.3 1.0 fusion.30
  8.3 0.0 copy-start.5
  8.3 1.1 negate_convert_fusion
  9.4 0.0 copy-start.6
  9.4 0.0 copy-start.7
  9.4 0.7 compare_select_fusion.1
  10.1 0.7 scatter_custom_fusion
  10.8 0.8 fusion.54
  11.6 0.0 copy-done
  11.6 1.1 fusion.8
  12.7 23.2 %all-gather = bf16[16,2,512]{2,1,0:T(2,128)(2,1)S(1)} all-gather(bf16[1,2,512]{2,1,0:T(2,128)(2,1)S(1)} %bitcast.34), channel_id=1, replica_groups=mesh['groups'=2,'freq'=16] {'freq'}, dimensions={0}, use_global_device_ids=true | all-gather | bytes 34816 | tf_op jit(solution)/shard_map/all_gather | solution.py:116
  35.9 0.0 copy-done.9
  35.9 0.6 gather_fusion
  36.5 0.0 copy-done.1
  36.5 0.2 fusion.55
  36.7 0.2 multiply_convert_fusion
  36.9 0.6 fusion.34
  37.4 0.2 subtract_convert_fusion.1
  37.7 0.0 copy-start.4
  37.7 0.0 copy-start.10
  37.7 1.0 add_convert_fusion
  38.7 0.0 copy-done.4
  38.7 0.3 copy-done.10
  39.0 0.6 fusion.7
  39.6 1.6 fusion.21
  41.2 0.6 convolution_add_fusion.1
  41.8 0.0 copy-start.2
  41.8 0.0 copy-done.5
  41.8 0.0 copy-done.6
  41.8 0.0 copy-done.7
  41.8 1.2 fusion.17
  43.1 0.0 copy-done.2
  43.1 0.0 copy-start.11
  43.1 0.4 add_reduce_fusion
  43.5 0.2 copy-done.11
  43.7 0.6 dynamic-slice
  45.0 2.3 convolution_add_fusion
  47.2 0.0 copy-start.8
  47.3 0.3 multiply_reduce_fusion
  47.6 0.6 gather_fusion.1
  48.2 59.2 %all-reduce.1 = (bf16[32,512]{1,0:T(8,128)(2,1)S(1)}, f32[2,256]{1,0:T(2,128)}) all-reduce(f32[32,512]{1,0:T(8,128)S(1)} %gather_fusion.1, f32[2,256]{1,0:T(2,128)S(1)} %pad_maximum_fusion.4), channel_id=2, replica_groups=mesh['groups'=2,'freq'=16] {'freq'}, use_global_device_ids=true, to_apply=%region_1.2.clone | all-reduce | flops 16896 | bytes 102400
  107.4 1.3 fusion.53
  108.7 0.0 copy-done.8
  108.7 3.0 %convolution_bitcast_fusion = f32[2048,512]{0,1:T(8,128)} fusion(bf16[2,2048]{1,0:T(2,128)(2,1)S(1)} %copy-done.8, bf16[512,512]{1,0:T(8,128)(2,1)S(1)} %copy-done.1, bf16[2,512]{1,0:T(2,128)(2,1)S(1)} %fusion.8, bf16[32,512]{1,0:T(8,128)(2,1)S(1)} %get-tuple-element.14, u32[]{:T(128)S(6)} %multiply.6), kind=kOutput, calls=%fused_computation.3 | convolution fusion | flops 5248000 | bytes 4730884 | tf_op jit(solution)/shard_map/dot_general | solution.py:92
  111.7 0.0 all-reduce.5.cloned.1.call-update
  111.8 137.2 %all-reduce.5.cloned.1.call-done = (f32[2048,512]{0,1:T(8,128)}, f32[512,512]{1,0:T(8,128)}, f32[512,512]{1,0:T(8,128)}) async-done(((f32[2048,512]{0,1:T(8,128)}, f32[512,512]{1,0:T(8,128)}, f32[512,512]{1,0:T(8,128)}), (f32[2048,512]{0,1:T(8,128)}, f32[512,512]{1,0:T(8,128)}, f32[512,512]{1,0:T(8,128)})) %all-reduce.5.cloned.1.call-update) | async-done | bytes 6291472 | tf_op jit(solution)/shard_map/psum | solution.py:139
  248.9 5.3 %copy.13 = f32[2048,512]{1,0:T(8,128)} copy(f32[2048,512]{0,1:T(8,128)} %get-tuple-element.16) | data formatting | bytes 8388608
  254.3 0.0 copy-start.3
  254.3 2.4 copy.25
  256.6 0.0 copy-done.3
  256.6 1.0 copy.26
  (7 shorter events, 0.1 us)
Async XLA Ops:
  7.2 4.4 %copy-start = (bf16[2048,512]{1,0:T(8,128)(2,1)S(1)}, bf16[2048,512]{1,0:T(8,128)(2,1)}, u32[]{:S(2)}) copy-start(bf16[2048,512]{1,0:T(8,128)(2,1)} %param.11) | copy-start | bytes 6291460
  7.2 28.7 %copy-start.9 = (bf16[24,512]{1,0:T(8,128)(2,1)S(1)}, bf16[24,512]{1,0:T(8,128)(2,1)}, u32[]{:S(2)}) copy-start(bf16[24,512]{1,0:T(8,128)(2,1)} %param.13) | copy-start | bytes 73732
  7.2 29.3 %copy-start.1 = (bf16[512,512]{1,0:T(8,128)(2,1)S(1)}, bf16[512,512]{1,0:T(8,128)(2,1)}, u32[]{:S(2)}) copy-start(bf16[512,512]{1,0:T(8,128)(2,1)} %param.12) | copy-start | bytes 1572868
  7.2 241.7 %all-reduce.5.cloned.1.call-start = ((), (), s32[]{:S(2)}) async-start(), calls=%async_computation | async-start | bytes 12582912 | tf_op jit(solution)/shard_map/psum | solution.py:139
  8.3 33.6 %copy-start.5 = (bf16[256,256]{1,0:T(8,128)(2,1)}, bf16[256,256]{1,0:T(8,128)(2,1)S(1)}, u32[]{:S(2)}) copy-start(bf16[256,256]{1,0:T(8,128)(2,1)S(1)} %fusion.30) | copy-start | bytes 393220
  9.4 32.4 %copy-start.6 = (bf16[256,256]{1,0:T(8,128)(2,1)}, bf16[256,256]{1,0:T(8,128)(2,1)S(1)}, u32[]{:S(2)}) copy-start(bf16[256,256]{1,0:T(8,128)(2,1)S(1)} %get-tuple-element.31) | copy-start | bytes 393220
  9.4 32.4 %copy-start.7 = (bf16[256,256]{1,0:T(8,128)(2,1)}, bf16[256,256]{1,0:T(8,128)(2,1)S(1)}, u32[]{:S(2)}) copy-start(bf16[256,256]{1,0:T(8,128)(2,1)S(1)} %get-tuple-element.32) | copy-start | bytes 393220
  37.7 1.0 copy-start.4
  37.7 1.3 copy-start.10
  41.8 1.3 copy-start.2
  43.1 0.7 copy-start.11
  47.2 61.5 %copy-start.8 = (bf16[2,2048]{1,0:T(2,128)(2,1)S(1)}, bf16[2,2048]{1,0:T(2,128)(2,1)}, u32[]{:S(2)}) copy-start(bf16[2,2048]{1,0:T(2,128)(2,1)} %param.8) | copy-start | bytes 24580
  254.3 2.4 copy-start.3
Sparse Core Ops, SparseCore 0:
  111.9 136.9 all-reduce.4
where the time goes:
time: 265 us; the launch traced here: 264 us
  waiting for transfers between devices  137 us (52%)
  blocking collectives  82.4 us (31%)
  between operations  14.9 us (6%)
  matrix products  13.4 us (5%)
  local copies, waits for them, and re-layouts  12.5 us (5%)
  other arithmetic  3.97 us (1%)
    psum x1, waiting for transfers between devices, local(): lax.psum((grad_enc, grad_dec, grad_out, grad_filter), 'freq')  137 us
    unnamed x1, blocking collectives  59.2 us
    all_gather x1, blocking collectives, local(): all_codes = lax.all_gather(codes_own, 'freq', axis=0, tiled=True)  23.2 us
    unnamed x29, local copies, waits for them, and re-layouts  9.8 us
  transfers between devices with their start and end apart: 1, of which 1 were waited for; matrix products, arithmetic and copies ran while one was open for 0% of the time, Pallas kernels for 0%

commit v1 on v0

--- a/solution.py
+++ b/solution.py
@@ -113,7 +113,27 @@
     codes_own = jnp.tanh(
         jnp.dot(encoder_input, encoder_weight, preferred_element_type=jnp.float32)
     ).astype(jnp.bfloat16)
-    all_codes = lax.all_gather(codes_own, "freq", axis=0, tiled=True)
+    n_now = lax.psum(1, axis_name="freq")
+    y1 = lax.axis_index("freq")
+    far_arr, odd, current_arr = (n_now, y1, codes_own.shape[0])
+    inbox = [(q, (q + 1) % far_arr) for q in range(far_arr)]
+    pile = [(q, (q - 1) % far_arr) for q in range(far_arr)]
+    all_codes = jnp.zeros(
+        (*codes_own.shape[:0], far_arr * current_arr, *codes_own.shape[1:]), codes_own.dtype
+    )
+    all_codes = lax.dynamic_update_slice_in_dim(all_codes, codes_own, odd * current_arr, axis=0)
+    shaped = t_next = codes_own
+    placed = far_arr // 2
+    for idx in range(1, placed + 1):
+        shaped = lax.ppermute(shaped, axis_name="freq", perm=inbox)
+        all_codes = lax.dynamic_update_slice_in_dim(
+            all_codes, shaped, (odd - idx) % far_arr * current_arr, axis=0
+        )
+        if idx < far_arr - placed:
+            t_next = lax.ppermute(t_next, "freq", perm=pile)
+            all_codes = lax.dynamic_update_slice_in_dim(
+                all_codes, t_next, (odd + idx) % far_arr * current_arr, axis=0
+            )
     inverse_ids = (
         jnp.zeros((samples,), jnp.int32).at[sample_index].set(jnp.arange(samples, dtype=jnp.int32))
     )

time: 265 us -> 289 us (1.091)
  starting transfers between devices: 0.04 us -> 32 us
  blocking collectives: 82.4 us -> 58.9 us
  waiting for transfers between devices: 137 us -> 155 us
    ppermute x0 -> x15, starting transfers between devices: none -> 32 us  [the longest x7 32 us: local(): t_next = lax.ppermute(t_next, 'freq', perm=pile)]
    all_gather x1 -> x0, blocking collectives: 23.2 us -> none  [local(): all_codes = lax.all_gather(codes_own, 'freq', axis=0, tiled=True)]
    ppermute x0 -> x15, waiting for transfers between devices: none -> 17.7 us  [the longest x8 11.4 us: local(): shaped = lax.ppermute(shaped, axis_name='freq', perm=inbox)]
    unnamed x29 -> x26, local copies, waits for them, and re-layouts: 9.8 us -> 10.4 us
  transfers between devices with their start and end apart: 1 -> 16, of which waited for: 1 -> 8; matrix products, arithmetic and copies ran while one was open for 0% -> 1% of each run, Pallas kernels for 0% -> 0%
where the time goes in v1:
time: 289 us
  waiting for transfers between devices  155 us (54%)
  blocking collectives  58.9 us (20%)
  starting transfers between devices  32 us (11%)
  between operations  15.1 us (5%)
  local copies, waits for them, and re-layouts  12.5 us (4%)
  matrix products  11.8 us (4%)
  other arithmetic  3.27 us (1%)
    psum x1, waiting for transfers between devices, local(): lax.psum((grad_enc, grad_dec, grad_out, grad_filter), 'freq')  137 us
    unnamed x1, blocking collectives  58.9 us
    ppermute x7, starting transfers between devices, local(): t_next = lax.ppermute(t_next, 'freq', perm=pile)  32 us
    ppermute x8, waiting for transfers between devices, local(): shaped = lax.ppermute(shaped, axis_name='freq', perm=inbox)  11.4 us
    unnamed x26, local copies, waits for them, and re-layouts  10.4 us
    ppermute x7, waiting for transfers between devices, local(): t_next = lax.ppermute(t_next, 'freq', perm=pile)  6.36 us
  transfers between devices with their start and end apart: 16, of which 8 were waited for; matrix products, arithmetic and copies ran while one was open for 1% of the time, Pallas kernels for 0%

profile of v1, /device:TPU:0, one launch (start us, length us, event | category | flops | bytes accessed | tf_op | source)
XLA Modules:
  0.0 288.6 jit_solution(1016130971863387611)
XLA Ops:
  7.2 0.0 copy-start
  7.2 0.0 all-reduce.5.cloned.1.call-start
  7.3 1.5 copy-done
  8.8 1.1 constant_dynamic-update-slice_fusion.15
  9.9 5.5 %collective-permute-start.1 = (bf16[2,512]{1,0:T(2,128)(2,1)S(1)}, bf16[2,512]{1,0:T(2,128)(2,1)S(1)}, u32[]{:S(2)}, u32[]{:S(2)}) collective-permute-start(bf16[2,512]{1,0:T(2,128)(2,1)S(1)} %get-tuple-element.30), channel_id=1, source_target_pairs={{0,15},{1,0},{2,1},{3,2},{4,3},{5,4},{6,5},{7,6},{8,7},{9,8},{10,9... | collective-permute-start | bytes 6152 | tf_op jit(solution)/shard_map/ppermute | solution.py:133
  15.4 0.0 collective-permute-start
  15.4 1.0 fusion.30
  16.4 1.1 negate_convert_fusion
  17.6 0.7 scatter_custom_fusion
  18.5 0.6 dynamic-slice
  19.7 0.0 collective-permute-done.1
  19.7 4.5 %collective-permute-start.3 = (bf16[2,512]{1,0:T(2,128)(2,1)S(1)}, bf16[2,512]{1,0:T(2,128)(2,1)S(1)}, u32[]{:S(2)}, u32[]{:S(2)}) collective-permute-start(bf16[2,512]{1,0:T(2,128)(2,1)S(1)} %collective-permute-done.1), channel_id=1, source_target_pairs={{0,15},{1,0},{2,1},{3,2},{4,3},{5,4},{6,5},{7,6},{8,7},{9,8},{10,9... | collective-permute-start | bytes 6152 | tf_op jit(solution)/shard_map/ppermute | solution.py:133
  24.2 0.0 collective-permute-done
  24.2 0.0 collective-permute-start.2
  24.2 1.3 collective-permute-done.3
  25.5 4.4 %collective-permute-start.5 = (bf16[2,512]{1,0:T(2,128)(2,1)S(1)}, bf16[2,512]{1,0:T(2,128)(2,1)S(1)}, u32[]{:S(2)}, u32[]{:S(2)}) collective-permute-start(bf16[2,512]{1,0:T(2,128)(2,1)S(1)} %collective-permute-done.3), channel_id=1, source_target_pairs={{0,15},{1,0},{2,1},{3,2},{4,3},{5,4},{6,5},{7,6},{8,7},{9,8},{10,9... | collective-permute-start | bytes 6152 | tf_op jit(solution)/shard_map/ppermute | solution.py:133
  29.9 0.0 collective-permute-done.2
  29.9 0.0 collective-permute-start.4
  29.9 1.3 collective-permute-done.5
  31.2 4.4 %collective-permute-start.7 = (bf16[2,512]{1,0:T(2,128)(2,1)S(1)}, bf16[2,512]{1,0:T(2,128)(2,1)S(1)}, u32[]{:S(2)}, u32[]{:S(2)}) collective-permute-start(bf16[2,512]{1,0:T(2,128)(2,1)S(1)} %collective-permute-done.5), channel_id=1, source_target_pairs={{0,15},{1,0},{2,1},{3,2},{4,3},{5,4},{6,5},{7,6},{8,7},{9,8},{10,9... | collective-permute-start | bytes 6152 | tf_op jit(solution)/shard_map/ppermute | solution.py:133
  35.6 0.0 collective-permute-done.4
  35.6 0.0 collective-permute-start.6
  35.6 1.3 collective-permute-done.7
  36.9 4.4 %collective-permute-start.9 = (bf16[2,512]{1,0:T(2,128)(2,1)S(1)}, bf16[2,512]{1,0:T(2,128)(2,1)S(1)}, u32[]{:S(2)}, u32[]{:S(2)}) collective-permute-start(bf16[2,512]{1,0:T(2,128)(2,1)S(1)} %collective-permute-done.7), channel_id=1, source_target_pairs={{0,15},{1,0},{2,1},{3,2},{4,3},{5,4},{6,5},{7,6},{8,7},{9,8},{10,9... | collective-permute-start | bytes 6152 | tf_op jit(solution)/shard_map/ppermute | solution.py:133
  41.3 0.0 collective-permute-done.6
  41.3 0.0 collective-permute-start.8
  41.4 1.3 collective-permute-done.9
  42.6 4.4 %collective-permute-start.11 = (bf16[2,512]{1,0:T(2,128)(2,1)S(1)}, bf16[2,512]{1,0:T(2,128)(2,1)S(1)}, u32[]{:S(2)}, u32[]{:S(2)}) collective-permute-start(bf16[2,512]{1,0:T(2,128)(2,1)S(1)} %collective-permute-done.9), channel_id=1, source_target_pairs={{0,15},{1,0},{2,1},{3,2},{4,3},{5,4},{6,5},{7,6},{8,7},{9,8},{10,9... | collective-permute-start | bytes 6152 | tf_op jit(solution)/shard_map/ppermute | solution.py:133
  47.0 0.0 collective-permute-done.8
  47.0 0.0 collective-permute-start.10
  47.1 1.3 collective-permute-done.11
  48.3 4.4 %collective-permute-start.13 = (bf16[2,512]{1,0:T(2,128)(2,1)S(1)}, bf16[2,512]{1,0:T(2,128)(2,1)S(1)}, u32[]{:S(2)}, u32[]{:S(2)}) collective-permute-start(bf16[2,512]{1,0:T(2,128)(2,1)S(1)} %collective-permute-done.11), channel_id=1, source_target_pairs={{0,15},{1,0},{2,1},{3,2},{4,3},{5,4},{6,5},{7,6},{8,7},{9,8},{10,9... | collective-permute-start | bytes 6152 | tf_op jit(solution)/shard_map/ppermute | solution.py:133
  52.7 0.0 collective-permute-done.10
  52.8 5.7 %collective-permute-done.12 = bf16[2,512]{1,0:T(2,128)(2,1)S(1)} collective-permute-done((bf16[2,512]{1,0:T(2,128)(2,1)S(1)}, bf16[2,512]{1,0:T(2,128)(2,1)S(1)}, u32[]{:S(2)}, u32[]{:S(2)}) %collective-permute-start.12) | collective-permute-done | bytes 2080 | tf_op jit(solution)/shard_map/ppermute | solution.py:128
  58.5 0.0 collective-permute-done.13
  58.5 5.7 %collective-permute-done.14 = bf16[2,512]{1,0:T(2,128)(2,1)S(1)} collective-permute-done((bf16[2,512]{1,0:T(2,128)(2,1)S(1)}, bf16[2,512]{1,0:T(2,128)(2,1)S(1)}, u32[]{:S(2)}, u32[]{:S(2)}) %collective-permute-start.14) | collective-permute-done | bytes 2080 | tf_op jit(solution)/shard_map/ppermute | solution.py:128
  64.2 0.6 gather_fusion
  64.8 0.2 fusion.55
  65.0 0.2 multiply_convert_fusion
  65.2 0.6 fusion.34
  65.7 0.2 subtract_convert_fusion.1
  66.0 0.0 copy-start.4
  66.0 0.0 copy-start.8
  66.0 1.0 add_convert_fusion
  67.0 0.0 copy-done.4
  67.0 0.3 copy-done.8
  67.3 0.6 fusion.7
  67.9 1.6 fusion.21
  69.5 0.6 convolution_add_fusion.1
  70.1 1.2 fusion.17
  71.3 0.4 add_reduce_fusion
  71.8 0.6 convolution_add_fusion
  72.4 0.0 copy-start.5
  72.4 0.3 multiply_reduce_fusion
  72.7 0.6 gather_fusion.1
  73.3 58.9 %all-reduce.1 = (bf16[32,512]{1,0:T(8,128)(2,1)S(1)}, f32[2,256]{1,0:T(2,128)}) all-reduce(f32[32,512]{1,0:T(8,128)S(1)} %gather_fusion.1, f32[2,256]{1,0:T(2,128)S(1)} %pad_maximum_fusion.4), channel_id=2, replica_groups=mesh['groups'=2,'freq'=16] {'freq'}, use_global_device_ids=true, to_apply=%region_1.2.clone | all-reduce | flops 16896 | bytes 102400
  132.2 1.3 fusion.53
  133.6 3.0 %convolution_bitcast_fusion = f32[2048,512]{0,1:T(8,128)} fusion(bf16[2,2048]{1,0:T(2,128)(2,1)S(1)} %copy-done.5, bf16[512,512]{1,0:T(8,128)(2,1)S(1)} %copy-done.1, bf16[2,512]{1,0:T(2,128)(2,1)S(1)} %get-tuple-element.30, bf16[32,512]{1,0:T(8,128)(2,1)S(1)} %get-tuple-element.14, u32[]{:T(128)S(6)} %multiply.6), kind=kOutput, calls=%fused_computation.3 | convolution fusion | flops 5248000 | bytes 4730884 | tf_op jit(solution)/shard_map/dot_general | solution.py:92
  136.6 0.0 all-reduce.5.cloned.1.call-update
  136.6 137.2 %all-reduce.5.cloned.1.call-done = (f32[2048,512]{0,1:T(8,128)}, f32[512,512]{1,0:T(8,128)}, f32[512,512]{1,0:T(8,128)}) async-done(((f32[2048,512]{0,1:T(8,128)}, f32[512,512]{1,0:T(8,128)}, f32[512,512]{1,0:T(8,128)}), (f32[2048,512]{0,1:T(8,128)}, f32[512,512]{1,0:T(8,128)}, f32[512,512]{1,0:T(8,128)})) %all-reduce.5.cloned.1.call-update) | async-done | bytes 6291472 | tf_op jit(solution)/shard_map/psum | solution.py:159
  273.8 5.4 %copy.13 = f32[2048,512]{1,0:T(8,128)} copy(f32[2048,512]{0,1:T(8,128)} %get-tuple-element.16) | data formatting | bytes 8388608
  279.2 1.0 copy.41
  280.2 0.6 copy-done.2
  280.8 1.0 copy.42
  (40 shorter events, 0.3 us)
Async XLA Ops:
  7.2 1.6 copy-start
  7.2 10.3 %copy-start.9 = (s32[32]{0:T(128)S(1)}, s32[32]{0:T(128)}, u32[]{:S(2)}) copy-start(s32[32]{0:T(128)} %param.10) | copy-start | bytes 388
  7.2 11.1 %copy-start.7 = (f32[2,256]{1,0:T(2,128)S(1)}, f32[2,256]{1,0:T(2,128)}, u32[]{:S(2)}) copy-start(f32[2,256]{1,0:T(2,128)} %param.14) | copy-start | bytes 6148
  7.2 11.1 %copy-start.6 = (bf16[24,512]{1,0:T(8,128)(2,1)S(1)}, bf16[24,512]{1,0:T(8,128)(2,1)}, u32[]{:S(2)}) copy-start(bf16[24,512]{1,0:T(8,128)(2,1)} %param.13) | copy-start | bytes 73732
  7.2 266.5 %all-reduce.5.cloned.1.call-start = ((), (), s32[]{:S(2)}) async-start(), calls=%async_computation | async-start | bytes 12582912 | tf_op jit(solution)/shard_map/psum | solution.py:159
  8.8 9.7 %copy-start.10 = (u32[32]{0:T(128)S(1)}, u32[32]{0:T(128)}, u32[]{:S(2)}) copy-start(u32[32]{0:T(128)} %constant.154) | copy-start | bytes 388
  8.8 56.0 %copy-start.1 = (bf16[512,512]{1,0:T(8,128)(2,1)S(1)}, bf16[512,512]{1,0:T(8,128)(2,1)}, u32[]{:S(2)}) copy-start(bf16[512,512]{1,0:T(8,128)(2,1)} %param.12) | copy-start | bytes 1572868
  9.9 9.8 %collective-permute-start.1 = (bf16[2,512]{1,0:T(2,128)(2,1)S(1)}, bf16[2,512]{1,0:T(2,128)(2,1)S(1)}, u32[]{:S(2)}, u32[]{:S(2)}) collective-permute-start(bf16[2,512]{1,0:T(2,128)(2,1)S(1)} %get-tuple-element.30), channel_id=1, source_target_pairs={{0,15},{1,0},{2,1},{3,2},{4,3},{5,4},{6,5},{7,6},{8,7},{9,8},{10,9... | collective-permute-start | bytes 6152 | tf_op jit(solution)/shard_map/ppermute | solution.py:133
  15.4 8.8 %collective-permute-start = (bf16[2,512]{1,0:T(2,128)(2,1)S(1)}, bf16[2,512]{1,0:T(2,128)(2,1)S(1)}, u32[]{:S(2)}, u32[]{:S(2)}) collective-permute-start(bf16[2,512]{1,0:T(2,128)(2,1)S(1)} %get-tuple-element.30), channel_id=1, source_target_pairs={{0,1},{1,2},{2,3},{3,4},{4,5},{5,6},{6,7},{7,8},{8,9},{9,10},{10,1... | collective-permute-start | bytes 6152 | tf_op jit(solution)/shard_map/ppermute | solution.py:128
  19.7 5.8 %collective-permute-start.3 = (bf16[2,512]{1,0:T(2,128)(2,1)S(1)}, bf16[2,512]{1,0:T(2,128)(2,1)S(1)}, u32[]{:S(2)}, u32[]{:S(2)}) collective-permute-start(bf16[2,512]{1,0:T(2,128)(2,1)S(1)} %collective-permute-done.1), channel_id=1, source_target_pairs={{0,15},{1,0},{2,1},{3,2},{4,3},{5,4},{6,5},{7,6},{8,7},{9,8},{10,9... | collective-permute-start | bytes 6152 | tf_op jit(solution)/shard_map/ppermute | solution.py:133
  24.2 5.7 %collective-permute-start.2 = (bf16[2,512]{1,0:T(2,128)(2,1)S(1)}, bf16[2,512]{1,0:T(2,128)(2,1)S(1)}, u32[]{:S(2)}, u32[]{:S(2)}) collective-permute-start(bf16[2,512]{1,0:T(2,128)(2,1)S(1)} %collective-permute-done), channel_id=1, source_target_pairs={{0,1},{1,2},{2,3},{3,4},{4,5},{5,6},{6,7},{7,8},{8,9},{9,10},{10,1... | collective-permute-start | bytes 6152 | tf_op jit(solution)/shard_map/ppermute | solution.py:128
  25.5 5.7 %collective-permute-start.5 = (bf16[2,512]{1,0:T(2,128)(2,1)S(1)}, bf16[2,512]{1,0:T(2,128)(2,1)S(1)}, u32[]{:S(2)}, u32[]{:S(2)}) collective-permute-start(bf16[2,512]{1,0:T(2,128)(2,1)S(1)} %collective-permute-done.3), channel_id=1, source_target_pairs={{0,15},{1,0},{2,1},{3,2},{4,3},{5,4},{6,5},{7,6},{8,7},{9,8},{10,9... | collective-permute-start | bytes 6152 | tf_op jit(solution)/shard_map/ppermute | solution.py:133
  29.9 5.7 %collective-permute-start.4 = (bf16[2,512]{1,0:T(2,128)(2,1)S(1)}, bf16[2,512]{1,0:T(2,128)(2,1)S(1)}, u32[]{:S(2)}, u32[]{:S(2)}) collective-permute-start(bf16[2,512]{1,0:T(2,128)(2,1)S(1)} %collective-permute-done.2), channel_id=1, source_target_pairs={{0,1},{1,2},{2,3},{3,4},{4,5},{5,6},{6,7},{7,8},{8,9},{9,10},{10,1... | collective-permute-start | bytes 6152 | tf_op jit(solution)/shard_map/ppermute | solution.py:128
  31.2 5.7 %collective-permute-start.7 = (bf16[2,512]{1,0:T(2,128)(2,1)S(1)}, bf16[2,512]{1,0:T(2,128)(2,1)S(1)}, u32[]{:S(2)}, u32[]{:S(2)}) collective-permute-start(bf16[2,512]{1,0:T(2,128)(2,1)S(1)} %collective-permute-done.5), channel_id=1, source_target_pairs={{0,15},{1,0},{2,1},{3,2},{4,3},{5,4},{6,5},{7,6},{8,7},{9,8},{10,9... | collective-permute-start | bytes 6152 | tf_op jit(solution)/shard_map/ppermute | solution.py:133
  35.6 5.7 %collective-permute-start.6 = (bf16[2,512]{1,0:T(2,128)(2,1)S(1)}, bf16[2,512]{1,0:T(2,128)(2,1)S(1)}, u32[]{:S(2)}, u32[]{:S(2)}) collective-permute-start(bf16[2,512]{1,0:T(2,128)(2,1)S(1)} %collective-permute-done.4), channel_id=1, source_target_pairs={{0,1},{1,2},{2,3},{3,4},{4,5},{5,6},{6,7},{7,8},{8,9},{9,10},{10,1... | collective-permute-start | bytes 6152 | tf_op jit(solution)/shard_map/ppermute | solution.py:128
  36.9 5.7 %collective-permute-start.9 = (bf16[2,512]{1,0:T(2,128)(2,1)S(1)}, bf16[2,512]{1,0:T(2,128)(2,1)S(1)}, u32[]{:S(2)}, u32[]{:S(2)}) collective-permute-start(bf16[2,512]{1,0:T(2,128)(2,1)S(1)} %collective-permute-done.7), channel_id=1, source_target_pairs={{0,15},{1,0},{2,1},{3,2},{4,3},{5,4},{6,5},{7,6},{8,7},{9,8},{10,9... | collective-permute-start | bytes 6152 | tf_op jit(solution)/shard_map/ppermute | solution.py:133
  41.3 5.7 %collective-permute-start.8 = (bf16[2,512]{1,0:T(2,128)(2,1)S(1)}, bf16[2,512]{1,0:T(2,128)(2,1)S(1)}, u32[]{:S(2)}, u32[]{:S(2)}) collective-permute-start(bf16[2,512]{1,0:T(2,128)(2,1)S(1)} %collective-permute-done.6), channel_id=1, source_target_pairs={{0,1},{1,2},{2,3},{3,4},{4,5},{5,6},{6,7},{7,8},{8,9},{9,10},{10,1... | collective-permute-start | bytes 6152 | tf_op jit(solution)/shard_map/ppermute | solution.py:128
  42.6 5.7 %collective-permute-start.11 = (bf16[2,512]{1,0:T(2,128)(2,1)S(1)}, bf16[2,512]{1,0:T(2,128)(2,1)S(1)}, u32[]{:S(2)}, u32[]{:S(2)}) collective-permute-start(bf16[2,512]{1,0:T(2,128)(2,1)S(1)} %collective-permute-done.9), channel_id=1, source_target_pairs={{0,15},{1,0},{2,1},{3,2},{4,3},{5,4},{6,5},{7,6},{8,7},{9,8},{10,9... | collective-permute-start | bytes 6152 | tf_op jit(solution)/shard_map/ppermute | solution.py:133
  47.0 5.7 %collective-permute-start.10 = (bf16[2,512]{1,0:T(2,128)(2,1)S(1)}, bf16[2,512]{1,0:T(2,128)(2,1)S(1)}, u32[]{:S(2)}, u32[]{:S(2)}) collective-permute-start(bf16[2,512]{1,0:T(2,128)(2,1)S(1)} %collective-permute-done.8), channel_id=1, source_target_pairs={{0,1},{1,2},{2,3},{3,4},{4,5},{5,6},{6,7},{7,8},{8,9},{9,10},{10,1... | collective-permute-start | bytes 6152 | tf_op jit(solution)/shard_map/ppermute | solution.py:128
  48.3 10.1 %collective-permute-start.13 = (bf16[2,512]{1,0:T(2,128)(2,1)S(1)}, bf16[2,512]{1,0:T(2,128)(2,1)S(1)}, u32[]{:S(2)}, u32[]{:S(2)}) collective-permute-start(bf16[2,512]{1,0:T(2,128)(2,1)S(1)} %collective-permute-done.11), channel_id=1, source_target_pairs={{0,15},{1,0},{2,1},{3,2},{4,3},{5,4},{6,5},{7,6},{8,7},{9,8},{10,9... | collective-permute-start | bytes 6152 | tf_op jit(solution)/shard_map/ppermute | solution.py:133
  52.7 5.7 %collective-permute-start.12 = (bf16[2,512]{1,0:T(2,128)(2,1)S(1)}, bf16[2,512]{1,0:T(2,128)(2,1)S(1)}, u32[]{:S(2)}, u32[]{:S(2)}) collective-permute-start(bf16[2,512]{1,0:T(2,128)(2,1)S(1)} %collective-permute-done.10), channel_id=1, source_target_pairs={{0,1},{1,2},{2,3},{3,4},{4,5},{5,6},{6,7},{7,8},{8,9},{9,10},{10,1... | collective-permute-start | bytes 6152 | tf_op jit(solution)/shard_map/ppermute | solution.py:128
  58.4 5.7 %collective-permute-start.14 = (bf16[2,512]{1,0:T(2,128)(2,1)S(1)}, bf16[2,512]{1,0:T(2,128)(2,1)S(1)}, u32[]{:S(2)}, u32[]{:S(2)}) collective-permute-start(bf16[2,512]{1,0:T(2,128)(2,1)S(1)} %collective-permute-done.12), channel_id=1, source_target_pairs={{0,1},{1,2},{2,3},{3,4},{4,5},{5,6},{6,7},{7,8},{8,9},{9,10},{10,1... | collective-permute-start | bytes 6152 | tf_op jit(solution)/shard_map/ppermute | solution.py:128
  66.0 1.0 copy-start.4
  66.0 1.3 copy-start.8
  72.4 61.2 %copy-start.5 = (bf16[2,2048]{1,0:T(2,128)(2,1)S(1)}, bf16[2,2048]{1,0:T(2,128)(2,1)}, u32[]{:S(2)}) copy-start(bf16[2,2048]{1,0:T(2,128)(2,1)} %param.8) | copy-start | bytes 24580
  273.8 5.4 %copy-start.3 = (f32[512,512]{1,0:T(8,128)S(1)}, f32[512,512]{1,0:T(8,128)}, u32[]{:S(2)}) copy-start(f32[512,512]{1,0:T(8,128)} %get-tuple-element.36) | copy-start | bytes 3145732
  279.2 1.6 copy-start.2
Sparse Core Ops, SparseCore 0:
  136.7 136.9 all-reduce.4
